TPU v7x, 256 devices: a whole 4x4x8 slice. The times are simulated.
256 devices in a mesh: seq: 64 (over x, z, core), tensor: 4 (over y).
Axes of the slice: x: 4, y: 4, z: 8, core: 2. Of those that a mesh axis runs over, the one named last changes fastest.
Arguments:
- hidden: bfloat16 [512, 1280], P('seq', 'tensor'), may hold values from -20 to 20
- inward_weight: bfloat16 [1280, 3, 1280], P(None, None, 'tensor'), may hold values from -0.15625 to 0.15625
- output_weight: bfloat16 [1280, 1280], P('tensor'), may hold values from -0.559017 to 0.559017
- score_gain: float32 [1280], P('tensor'), may hold values from 0.5 to 9
- eigen_rate: float32 [1280], replicated, may hold values from 0.1 to 0.6
- lengths: int32 [512], replicated, may hold values from 1 to 16384, as said below
- page_request: int32 [1536], P('seq'), may hold values from 0 to 511, as said below
- page_number: int32 [1536], P('seq'), may hold values from 0 to 128, as said below
- page_cache: bfloat16 [1536, 128, 2, 1280], P('seq', None, None, 'tensor'), may hold values from -6 to 6
Outputs:
- new_hidden: bfloat16 [512, 1280], P('seq', 'tensor')
Inputs may be any that keep to these rules, and one draw needn't show every extreme that they name: `lengths`: exactly 4 requests have more than 256 cached positions; they have more than 16256, one has exactly 16384. Every other request has at most 256, one exactly 256. `page_request`: each page of each request stands in exactly one slot: pages 0 to 1 of every short request, pages 0 to 127 of every long request. The remaining 2 * 4 slots name a long request with page number 128 and hold nothing live. `page_number`: see page_request.
All inputs are finite; a program needn't handle non-finite values.
Results may differ from a plain program's by a relative error of at most 0.012.
The roundings to bfloat16 on the way count: a program that leaves them out, or rounds other values in their place, can miss the bound.
Values may be sent and summed in bfloat16 or wider, within the bound.
No kernel may reach another device: no remote copies, remote signals or barrier semaphores. Data moves between devices by JAX's collectives and lax.ppermute only.
A program may use at most 192 MiB of HBM per device.

v0:
```python
import math
import jax
import jax.numpy as jnp
from jax import lax
from jax.sharding import PartitionSpec as P

HEAD_DIM = 64
epsilon = 1e-06
far_below = -1e30


def head_norm(values, gain):
    shaped = values.reshape(values.shape[:-1] + (-1, HEAD_DIM))
    normed = shaped / jnp.sqrt(jnp.mean(shaped * shaped, axis=-1, keepdims=True) + epsilon)
    return normed * gain.reshape(-1, HEAD_DIM)


def scale_heads(summed, factor):
    shaped = summed.reshape(summed.shape[:-1] + (factor.shape[-1], -1))
    return (shaped * factor[..., None]).reshape(summed.shape)


def local(
    hidden,
    inward_weight,
    output_weight,
    score_gain,
    eigen_rate,
    lengths,
    page_request,
    page_number,
    page_cache,
):
    rows, width_local = hidden.shape
    heads_local = width_local // HEAD_DIM
    gathered = lax.all_gather(hidden, "tensor", axis=1, tiled=True)
    projected = jnp.dot(
        gathered,
        inward_weight.reshape(inward_weight.shape[0], -1),
        preferred_element_type=jnp.float32,
    )
    query = head_norm(projected[:, :width_local], score_gain).astype(jnp.bfloat16)
    key_new = head_norm(projected[:, width_local : 2 * width_local], score_gain).astype(
        jnp.bfloat16
    )
    value_own = projected[:, 2 * width_local :].astype(jnp.bfloat16)
    own_score = jnp.sum(
        (query.astype(jnp.float32) * key_new.astype(jnp.float32)).reshape(
            rows, heads_local, HEAD_DIM
        ),
        axis=-1,
    ) / math.sqrt(HEAD_DIM)
    all_queries = lax.all_gather(query, "seq", axis=0, tiled=True)
    pages, page_len = (page_cache.shape[0], page_cache.shape[1])
    owner_query = all_queries[page_request].reshape(pages, heads_local, HEAD_DIM)
    keys_scaled = head_norm(page_cache[:, :, 0, :].astype(jnp.float32), score_gain).astype(
        jnp.bfloat16
    )
    values_paged = page_cache[:, :, 1, :].reshape(pages, page_len, heads_local, HEAD_DIM)
    scores = jnp.einsum(
        "sphd,shd->shp", keys_scaled, owner_query, preferred_element_type=jnp.float32
    ) / math.sqrt(HEAD_DIM)
    positions = page_number[:, None] * page_len + jnp.arange(page_len, dtype=jnp.int32)[None, :]
    live_mask = positions < lengths[page_request][:, None]
    page_max = jnp.max(jnp.where(live_mask[:, None, :], scores, far_below), axis=-1)
    weights = jnp.where(live_mask[:, None, :], jnp.exp(scores - page_max[..., None]), 0.0).astype(
        jnp.bfloat16
    )
    page_total = jnp.sum(weights.astype(jnp.float32), axis=-1)
    page_acc = jnp.einsum(
        "shp,sphd->shd", weights, values_paged, preferred_element_type=jnp.float32
    ).reshape(pages, width_local)
    packed = jnp.concatenate(
        [page_acc, page_total, page_max, page_request.astype(jnp.float32)[:, None]], axis=1
    )
    all_parts = lax.all_gather(packed, "seq", axis=0, tiled=True)
    acc_all = all_parts[:, :width_local]
    total_all = all_parts[:, width_local : width_local + heads_local]
    max_all = all_parts[:, width_local + heads_local : width_local + 2 * heads_local]
    owner_all = all_parts[:, width_local + 2 * heads_local]
    first_row = lax.axis_index("seq") * rows
    row_ids = (first_row + jnp.arange(rows, dtype=jnp.int32)).astype(jnp.float32)
    mine = owner_all[None, :] == row_ids[:, None]
    masked_max = jnp.max(jnp.where(mine[:, :, None], max_all[None], far_below), axis=1)
    final_max = jnp.maximum(masked_max, own_score)
    factor = jnp.where(mine[:, :, None], jnp.exp(max_all[None] - final_max[:, None, :]), 0.0)
    own_factor = jnp.exp(own_score - final_max)
    total = jnp.sum(factor * total_all[None], axis=1) + own_factor
    stored = jnp.einsum(
        "rsh,shd->rhd",
        factor,
        acc_all.reshape(-1, heads_local, HEAD_DIM),
        precision=lax.Precision.HIGHEST,
    ).reshape(rows, width_local)
    summed = stored + scale_heads(value_own.astype(jnp.float32), own_factor)
    attended = (
        (summed.reshape(rows, heads_local, HEAD_DIM) / total[..., None])
        .reshape(rows, width_local)
        .astype(jnp.bfloat16)
    )
    partial_out = jnp.dot(attended, output_weight, preferred_element_type=jnp.float32)
    attn_out = lax.psum(partial_out, "tensor")
    width = attn_out.shape[1]
    state = gathered.astype(jnp.float32)
    unit = attn_out / jnp.sqrt(
        jnp.sum(attn_out * attn_out, axis=-1, keepdims=True) / width + epsilon
    )
    mixed = state + eigen_rate * (unit - state)
    result = mixed / jnp.sqrt(jnp.sum(mixed * mixed, axis=-1, keepdims=True) / width + epsilon)
    first_col = lax.axis_index("tensor") * width_local
    return lax.dynamic_slice_in_dim(result, first_col, width_local, 1).astype(jnp.bfloat16)


def solution(mesh):
    placed = (
        P("seq", "tensor"),
        P(None, None, "tensor"),
        P("tensor", None),
        P("tensor"),
        P(),
        P(),
        P("seq"),
        P("seq"),
        P("seq", None, None, "tensor"),
    )
    return jax.shard_map(
        local, mesh=mesh, in_specs=placed, out_specs=P("seq", "tensor"), check_vma=False
    )
```

profile of v0, /device:TPU:4, one launch (start us, length us, event | category | flops | bytes accessed | tf_op | source)
XLA Modules:
  0.0 202.5 jit_solution(14112942308790230901)
XLA Ops:
  6.5 0.8 broadcast_multiply_fusion
  7.3 0.7 compare_select_fusion
  8.1 0.8 mul.86
  8.8 12.7 %all-gather = bf16[4,320,8]{1,2,0:T(8,128)(2,1)S(1)} all-gather(bf16[1,320,8]{1,2,0:T(8,128)(2,1)} %bitcast.52), channel_id=1, replica_groups=mesh['seq'=64,'tensor'=4] {'tensor'}, dimensions={0}, use_global_device_ids=true | all-gather | bytes 25600 | tf_op jit(solution)/shard_map/all_gather | solution.py:36
  21.7 0.7 fusion.21
  22.5 0.6 copy-done.3
  23.6 53.2 %all_gather.10 = bf16[512,5,64]{2,0,1:T(8,128)(2,1)S(1)} all-gather(bf16[8,5,64]{2,0,1:T(8,128)(2,1)S(1)} %copy.50), channel_id=1, replica_groups=mesh['seq'=64,'tensor'=4] {'seq'}, dimensions={0}, use_global_device_ids=true | all-gather | bytes 332800 | tf_op jit(solution)/shard_map/all_gather | solution.py:53
  76.8 0.5 copy.51
  77.2 0.7 gather_fusion
  78.0 1.2 gather_fusion.1
  79.2 3.7 %fusion.18 = (bf16[24,128,1,320]{1,3,2,0:T(8,128)(2,1)}, bf16[24,128,1,320]{1,3,2,0:T(8,128)(2,1)S(1)}) fusion(bf16[24,128,2,320]{1,3,2,0:T(8,128)(2,1)} %param.17), kind=kLoop, calls=%fused_computation.58 | loop fusion | bytes 7864320 | tf_op jit(solution)/shard_map/slice | solution.py:59
  82.8 0.7 fusion
  83.7 0.7 fusion.3
  85.0 2.6 %fusion.9 = f32[24,5,1,64]{3,2,1,0:T(1,128)S(1)} fusion(bf16[24,128,5,64]{1,3,2,0:T(8,128)(2,1)} %bitcast.49, bf16[24,5,128,1]{2,0,1,3:T(8,128)(2,1)S(1)} %get-tuple-element.15), kind=kOutput, calls=%fused_computation.20 | convolution fusion | flops 1966080 | bytes 2027520 | tf_op jit(solution)/shard_map/shp,sphd->shd/dot_general | solution.py:70
  87.7 0.7 pad_maximum_fusion
  88.5 74.1 %all-gather.3.cloned.1.call-done = f32[1536,331]{1,0:T(8,128)} async-done(((f32[24,331]{1,0:T(8,128)}), f32[1536,331]{1,0:T(8,128)}) %all-gather.3.cloned.1.call-update) | async-done | bytes 2033680 | tf_op jit(solution)/shard_map/all_gather | solution.py:76
  162.7 3.0 %fusion.19 = (f32[1536,5]{1,0:T(8,128)}, f32[1536,5]{1,0:T(8,128)S(1)}) fusion(f32[1536,331]{1,0:T(8,128)} %all-gather.3.cloned.1.call-done), kind=kLoop, calls=%fused_computation.59 | loop fusion | bytes 122880 | tf_op jit(solution)/shard_map/slice | solution.py:79
  165.6 1.4 copy.56
  167.3 1.6 slice_reduce_fusion
  169.8 3.0 %copy.55 = f32[1536,320]{0,1:T(8,128)} copy(f32[1536,320]{1,0:T(8,128)} %bitcast.45) | data formatting | bytes 3932160 | tf_op jit(solution)/shard_map/slice | solution.py:77
  172.9 3.3 %convolution_bitcast_fusion = f32[8,5,64]{2,0,1:T(8,128)S(1)} fusion(f32[1536,5,64]{0,2,1:T(8,128)} %bitcast.46, f32[8,5]{0,1:T(8,128)S(1)} %multiply_maximum_fusion, f32[1536,5]{0,1:T(8,128)S(1)} %copy.56, pred[8,1536]{1,0:T(8,128)(4,1)S(1)} %broadcast_compare_fusion), kind=kOutput, calls=%fused_computation.8 | convolution fusion | flops 47308800 | bytes 2019488 | tf_op jit(solution)/shard_map/rsh,shd->rhd/dot_general | solution.py:89
  176.3 0.9 fusion.14
  177.2 17.4 %psum.7 = f32[8,1280]{1,0:T(8,128)S(1)} all-reduce(f32[8,1280]{1,0:T(8,128)S(1)} %fusion.14), channel_id=1, replica_groups=mesh['seq'=64,'tensor'=4] {'tensor'}, use_global_device_ids=true, to_apply=%region_8.9 | all-reduce | flops 10240 | bytes 81920 | tf_op jit(solution)/shard_map/psum | solution.py:102
  194.9 0.7 fusion.13
  (53 shorter events, 3.1 us)
Async XLA Ops:
  6.5 15.1 %copy-start = (bf16[1280,3,320]{0,2,1:T(8,128)(2,1)S(1)}, bf16[1280,3,320]{0,2,1:T(8,128)(2,1)}, u32[]{:S(2)}) copy-start(bf16[1280,3,320]{0,2,1:T(8,128)(2,1)} %param.10) | copy-start | bytes 7372804
  6.5 156.1 %all-gather.3.cloned.1.call-start = ((), (), s32[]{:S(2)}) async-start(), calls=%async_computation | async-start | bytes 2396160 | tf_op jit(solution)/shard_map/all_gather | solution.py:76
  21.6 55.6 %copy-start.1 = (s32[512]{0:T(512)S(1)}, s32[512]{0:T(512)}, u32[]{:S(2)}) copy-start(s32[512]{0:T(512)} %param.14) | copy-start | bytes 6148
  22.4 0.6 copy-start.3
  79.2 4.5 %copy-start.4 = (bf16[24,5,64]{2,1,0:T(8,128)(2,1)S(1)}, bf16[24,5,64]{2,1,0:T(8,128)(2,1)}, u32[]{:S(2)}) copy-start(bf16[24,5,64]{2,1,0:T(8,128)(2,1)} %gather_fusion.1) | copy-start | bytes 46084
  169.8 6.5 %copy-start.2 = (bf16[320,1280]{1,0:T(8,128)(2,1)S(1)}, bf16[320,1280]{1,0:T(8,128)(2,1)}, u32[]{:S(2)}) copy-start(bf16[320,1280]{1,0:T(8,128)(2,1)} %param.11) | copy-start | bytes 2457604
  172.9 21.8 %copy-start.5 = (f32[1280]{0:T(1024)S(1)}, f32[1280]{0:T(1024)}, u32[]{:S(2)}) copy-start(f32[1280]{0:T(1024)} %param.13) | copy-start | bytes 15364
Sparse Core Ops, SparseCore 0:
  88.6 74.0 all-gather.2
where the time goes:
time: 203 us; the launch traced here: 202 us
  blocking collectives  83.2 us (41%)
  waiting for transfers between devices  74.1 us (37%)
  local copies, waits for them, and re-layouts  18 us (9%)
  between operations  13.5 us (7%)
  matrix products  8.35 us (4%)
  other arithmetic  5.14 us (3%)
    all_gather x1, waiting for transfers between devices, local(): all_parts = lax.all_gather(packed, 'seq', axis=0, tiled=True)  74.1 us
    all_gather x1, blocking collectives, local(): all_queries = lax.all_gather(query, 'seq', axis=0, tiled=True)  53.2 us
    psum x1, blocking collectives, local(): attn_out = lax.psum(partial_out, 'tensor')  17.4 us
    all_gather x1, blocking collectives, local(): gathered = lax.all_gather(hidden, 'tensor', axis=1, tiled=True)  12.7 us
    slice x2, local copies, waits for them, and re-layouts, local(): all_parts[:, width_local + heads_local:width_local + 2 * heads_local]  4.38 us
  transfers between devices with their start and end apart: 1, of which 1 were waited for; matrix products, arithmetic and copies ran while one was open for 0% of the time, Pallas kernels for 0%

commit v1 on v0

--- a/solution.py
+++ b/solution.py
@@ -33,7 +33,16 @@
 ):
     rows, width_local = hidden.shape
     heads_local = width_local // HEAD_DIM
-    gathered = lax.all_gather(hidden, "tensor", axis=1, tiled=True)
+    ways = lax.axis_size("tensor")
+    up = [(d, (d + 1) % ways) for d in range(ways)]
+    down = [(d, (d - 1) % ways) for d in range(ways)]
+    earlier, later = ([hidden], [hidden])
+    for _ in range(ways // 2):
+        earlier.append(lax.ppermute(earlier[-1], "tensor", up))
+    for _ in range((ways - 1) // 2):
+        later.append(lax.ppermute(later[-1], "tensor", down))
+    line = jnp.concatenate([*earlier[::-1], *later[1:]], axis=1)
+    gathered = jnp.roll(line, (lax.axis_index("tensor") - ways // 2) * hidden.shape[1], axis=1)
     projected = jnp.dot(
         gathered,
         inward_weight.reshape(inward_weight.shape[0], -1),

time: 203 us -> 199 us (0.980)
  blocking collectives: 83.2 us -> 70.6 us
  starting transfers between devices: 0.01 us -> 3.68 us
    all_gather x1 -> x0, blocking collectives: 12.7 us -> none  [local(): gathered = lax.all_gather(hidden, 'tensor', axis=1, tiled=True)]
    ppermute x0 -> x3, starting transfers between devices: none -> 3.68 us  [the longest x2 2.02 us: local(): earlier.append(lax.ppermute(earlier[-1], 'tensor', up))]
    ppermute x0 -> x3, waiting for transfers between devices: none -> 3.64 us  [the longest x2 3.64 us: local(): earlier.append(lax.ppermute(earlier[-1], 'tensor', up))]
  transfers between devices with their start and end apart: 1 -> 4, of which waited for: 1 -> 2; matrix products, arithmetic and copies ran while one was open for 0% -> 4% of each run, Pallas kernels for 0% -> 0%
where the time goes in v1:
time: 199 us
  waiting for transfers between devices  76.1 us (38%)
  blocking collectives  70.6 us (35%)
  local copies, waits for them, and re-layouts  19.3 us (10%)
  between operations  13.6 us (7%)
  matrix products  9.88 us (5%)
  other arithmetic  5.63 us (3%)
  starting transfers between devices  3.68 us (2%)
    all_gather x1, waiting for transfers between devices, local(): all_parts = lax.all_gather(packed, 'seq', axis=0, tiled=True)  72.4 us
    all_gather x1, blocking collectives, local(): all_queries = lax.all_gather(query, 'seq', axis=0, tiled=True)  53.2 us
    psum x1, blocking collectives, local(): attn_out = lax.psum(partial_out, 'tensor')  17.4 us
    slice x2, local copies, waits for them, and re-layouts, local(): all_parts[:, width_local + heads_local:width_local + 2 * heads_local]  4.38 us
  transfers between devices with their start and end apart: 4, of which 2 were waited for; matrix products, arithmetic and copies ran while one was open for 4% of the time, Pallas kernels for 0%

profile of v1, /device:TPU:4, one launch (start us, length us, event | category | flops | bytes accessed | tf_op | source)
XLA Modules:
  0.0 198.7 jit_solution(1189798924399698099)
XLA Ops:
  6.5 1.6 collective-permute-start
  8.1 1.7 collective-permute-start.2
  10.4 0.7 compare_select_fusion
  11.2 3.7 %fusion.21 = (bf16[24,128,1,320]{1,3,2,0:T(8,128)(2,1)}, bf16[24,128,1,320]{1,3,2,0:T(8,128)(2,1)S(1)}) fusion(bf16[24,128,2,320]{1,3,2,0:T(8,128)(2,1)} %param.17), kind=kLoop, calls=%fused_computation.61 | loop fusion | bytes 7864320 | tf_op jit(solution)/shard_map/slice | solution.py:68
  14.9 1.3 copy-done.2
  16.1 0.7 fusion
  17.5 0.7 gather_fusion
  18.9 0.7 copy.48
  19.5 3.6 %collective-permute-done.1 = bf16[8,320]{1,0:T(8,128)(2,1)S(1)} collective-permute-done((bf16[8,320]{1,0:T(8,128)(2,1)S(1)}, bf16[8,320]{1,0:T(8,128)(2,1)S(1)}, u32[]{:S(2)}, u32[]{:S(2)}) %collective-permute-start.1) | collective-permute-done | bytes 5152 | tf_op jit(solution)/shard_map/ppermute | solution.py:41
  23.3 0.8 fusion.13
  25.2 53.2 %all_gather.6 = bf16[512,5,64]{2,0,1:T(8,128)(2,1)S(1)} all-gather(bf16[8,5,64]{2,0,1:T(8,128)(2,1)S(1)} %copy.44), channel_id=1, replica_groups=mesh['seq'=64,'tensor'=4] {'seq'}, dimensions={0}, use_global_device_ids=true | all-gather | bytes 332800 | tf_op jit(solution)/shard_map/all_gather | solution.py:62
  78.9 1.3 gather_fusion.1
  80.2 2.3 %fusion.3 = f32[24,5,1,128]{3,2,1,0:T(1,128)S(1)} fusion(bf16[24,128,5,64]{1,3,2,0:T(8,128)(2,1)} %bitcast.34, f32[5,64]{1,0:T(8,128)} %copy-done.7, f32[24,128,5]{1,2,0:T(8,128)} %add_sqrt_fusion, bf16[24,5,64,1]{2,1,0,3:T(8,128)(2,1)} %bitcast.37), kind=kOutput, calls=%fused_computation.7 | convolution fusion | flops 5898240 | bytes 2105600 | tf_op jit(solution)/shard_map/sphd,shd->shp/dot_general | solution.py:69
  82.9 2.6 %fusion.9 = f32[24,5,1,64]{3,2,1,0:T(1,128)S(1)} fusion(bf16[24,128,5,64]{1,3,2,0:T(8,128)(2,1)} %bitcast.35, bf16[24,5,128,1]{2,0,1,3:T(8,128)(2,1)S(1)} %get-tuple-element.15), kind=kOutput, calls=%fused_computation.20 | convolution fusion | flops 1966080 | bytes 2027520 | tf_op jit(solution)/shard_map/shp,sphd->shd/dot_general | solution.py:79
  85.7 0.7 pad_maximum_fusion
  86.5 72.4 %all-gather.2.cloned.1.call-done = f32[1536,331]{1,0:T(8,128)} async-done(((f32[24,331]{1,0:T(8,128)}), f32[1536,331]{1,0:T(8,128)}) %all-gather.2.cloned.1.call-update) | async-done | bytes 2033680 | tf_op jit(solution)/shard_map/all_gather | solution.py:85
  158.9 3.0 %fusion.22 = (f32[1536,5]{1,0:T(8,128)}, f32[1536,5]{1,0:T(8,128)S(1)}) fusion(f32[1536,331]{1,0:T(8,128)} %all-gather.2.cloned.1.call-done), kind=kLoop, calls=%fused_computation.62 | loop fusion | bytes 122880 | tf_op jit(solution)/shard_map/slice | solution.py:88
  161.9 1.4 copy.50
  163.6 1.6 slice_reduce_fusion
  166.1 3.0 %copy.49 = f32[1536,320]{0,1:T(8,128)} copy(f32[1536,320]{1,0:T(8,128)} %bitcast.31) | data formatting | bytes 3932160 | tf_op jit(solution)/shard_map/slice | solution.py:86
  169.1 3.3 %convolution_bitcast_fusion = f32[8,5,64]{2,0,1:T(8,128)S(1)} fusion(f32[1536,5,64]{0,2,1:T(8,128)} %bitcast.32, f32[8,5]{0,1:T(8,128)S(1)} %multiply_maximum_fusion, f32[1536,5]{0,1:T(8,128)S(1)} %copy.50, pred[8,1536]{1,0:T(8,128)(4,1)S(1)} %broadcast_compare_fusion), kind=kOutput, calls=%fused_computation.8 | convolution fusion | flops 47308800 | bytes 2019488 | tf_op jit(solution)/shard_map/rsh,shd->rhd/dot_general | solution.py:98
  172.6 0.9 fusion.16
  173.5 17.4 %psum.7 = f32[8,1280]{1,0:T(8,128)S(1)} all-reduce(f32[8,1280]{1,0:T(8,128)S(1)} %fusion.16), channel_id=1, replica_groups=mesh['seq'=64,'tensor'=4] {'tensor'}, use_global_device_ids=true, to_apply=%region_8.9 | all-reduce | flops 10240 | bytes 81920 | tf_op jit(solution)/shard_map/psum | solution.py:111
  191.2 0.7 fusion.15
  (67 shorter events, 5.9 us)
Async XLA Ops:
  6.5 16.7 %copy-start = (bf16[1280,3,320]{0,2,1:T(8,128)(2,1)S(1)}, bf16[1280,3,320]{0,2,1:T(8,128)(2,1)}, u32[]{:S(2)}) copy-start(bf16[1280,3,320]{0,2,1:T(8,128)(2,1)} %param.10) | copy-start | bytes 7372804
  6.5 152.4 %all-gather.2.cloned.1.call-start = ((), (), s32[]{:S(2)}) async-start(), calls=%async_computation | async-start | bytes 2396160 | tf_op jit(solution)/shard_map/all_gather | solution.py:85
  6.5 11.7 %collective-permute-start = (bf16[8,320]{1,0:T(8,128)(2,1)}, bf16[8,320]{1,0:T(8,128)(2,1)S(1)}, u32[]{:S(2)}, u32[]{:S(2)}) collective-permute-start(bf16[8,320]{1,0:T(8,128)(2,1)} %param.9), channel_id=1, source_target_pairs={{0,1},{1,2},{2,3},{3,0},{4,5},{5,6},{6,7},{7,4},{8,9},{9,10},{10,1... | collective-permute-start | bytes 15368 | tf_op jit(solution)/shard_map/ppermute | solution.py:41
  8.1 11.4 %collective-permute-start.2 = (bf16[8,320]{1,0:T(8,128)(2,1)}, bf16[8,320]{1,0:T(8,128)(2,1)S(1)}, u32[]{:S(2)}, u32[]{:S(2)}) collective-permute-start(bf16[8,320]{1,0:T(8,128)(2,1)} %param.9), channel_id=1, source_target_pairs={{0,3},{1,0},{2,1},{3,2},{4,7},{5,4},{6,5},{7,6},{8,11},{9,8},{10,9... | collective-permute-start | bytes 15368 | tf_op jit(solution)/shard_map/ppermute | solution.py:43
  14.8 1.3 copy-start.2
  14.8 2.7 %copy-start.1 = (s32[512]{0:T(512)S(1)}, s32[512]{0:T(512)}, u32[]{:S(2)}) copy-start(s32[512]{0:T(512)} %param.14) | copy-start | bytes 6148
  14.8 3.9 %copy-start.10 = (f32[320]{0:T(512)S(1)}, f32[320]{0:T(512)}, u32[]{:S(2)}) copy-start(f32[320]{0:T(512)} %param.12) | copy-start | bytes 3844
  14.8 8.3 %copy-start.6 = (bf16[8,320]{1,0:T(8,128)(2,1)S(1)}, bf16[8,320]{1,0:T(8,128)(2,1)}, u32[]{:S(2)}) copy-start(bf16[8,320]{1,0:T(8,128)(2,1)} %param.9) | copy-start | bytes 15364
  17.5 0.7 copy-start.9
  18.3 4.9 %collective-permute-start.1 = (bf16[8,320]{1,0:T(8,128)(2,1)S(1)}, bf16[8,320]{1,0:T(8,128)(2,1)S(1)}, u32[]{:S(2)}, u32[]{:S(2)}) collective-permute-start(bf16[8,320]{1,0:T(8,128)(2,1)S(1)} %collective-permute-done), channel_id=1, source_target_pairs={{0,1},{1,2},{2,3},{3,0},{4,5},{5,6},{6,7},{7,4},{8,9},{9,10},{10,1... | collective-permute-start | bytes 15368 | tf_op jit(solution)/shard_map/ppermute | solution.py:41
  18.9 6.3 %copy-start.7 = (f32[5,64]{1,0:T(8,128)}, f32[5,64]{1,0:T(8,128)S(1)}, u32[]{:S(2)}) copy-start(f32[5,64]{1,0:T(8,128)S(1)} %mul.90) | copy-start | bytes 3844
  24.0 0.6 copy-start.4
  82.5 3.2 %copy-start.5 = (f32[24,1]{1,0:T(8,128)S(1)}, f32[24,1]{1,0:T(8,128)}, u32[]{:S(2)}) copy-start(f32[24,1]{1,0:T(8,128)} %copy.48) | copy-start | bytes 292
  166.1 6.5 %copy-start.3 = (bf16[320,1280]{1,0:T(8,128)(2,1)S(1)}, bf16[320,1280]{1,0:T(8,128)(2,1)}, u32[]{:S(2)}) copy-start(bf16[320,1280]{1,0:T(8,128)(2,1)} %param.11) | copy-start | bytes 2457604
  169.1 21.8 %copy-start.8 = (f32[1280]{0:T(1024)S(1)}, f32[1280]{0:T(1024)}, u32[]{:S(2)}) copy-start(f32[1280]{0:T(1024)} %param.13) | copy-start | bytes 15364
Sparse Core Ops, SparseCore 0:
  86.5 72.3 all-gather.1
